TPU v7x, 512 devices: a whole 4x8x8 slice. The times are simulated.
512 devices in a mesh: tm: 16 (over z, y_hi), space: 32 (over x, y_lo, core).
Axes of the slice: x: 4, y: 8 (y_hi: 2, y_lo: 4; y = y_hi * 4 + y_lo), z: 8, core: 2. Of those that a mesh axis runs over, the one named last changes fastest.
Arguments:
- state: float32 [16, 5, 256, 32, 128], P('tm', None, 'space'), may hold values from -6 to 6
- base: float32 [16, 5, 256, 32, 128], P('tm', None, 'space'), may hold values from -6 to 6
- pseudo_step: float32 [256, 32, 128], P('space'), may hold values from 0.05 to 0.3
- eddy_visc: float32 [256, 32, 128], P('space'), may hold values from 0.02 to 0.2
- jacobians: float32 [3, 5, 5], replicated, may hold values from -2.5 to 2.5
- partner_radial: int32 [2, 256, 128], P(None, 'space'), may hold values from 0 to 127, each once within a row
- partner_instance: int32 [16, 2, 256, 128], P('tm', None, 'space'), may hold values from 0 to 15, as said below
Outputs:
- updated: float32 [16, 5, 256, 32, 128], P('tm', None, 'space')
Inputs may be any that keep to these rules, and one draw needn't show every extreme that they name: partner_radial[s, i, :] is a permutation of the radial indices 0..127: the partner cells on the opposite periodic face in the same axial plane. partner_instance[n, 0, i, k] = (n + L_i) mod 16 and partner_instance[n, 1, i, k] = (n - L_i) mod 16 for a lag L_i in 1..15 that depends only on the axial plane i.
All inputs are finite; a program needn't handle non-finite values.
Results may differ from a plain program's by a relative error of at most 0.00005.
Values sent between devices are 32-bit elements; how exact they have to be, the bound alone decides.
No kernel may reach another device: no remote copies, remote signals or barrier semaphores. Data moves between devices by JAX's collectives and lax.ppermute only.
A program may use at most 64 MiB of HBM per device.

v0:
```python
import math
import jax
import jax.numpy as jnp
from jax import lax
from jax.sharding import Mesh
from jax.sharding import PartitionSpec as P

SECTION_ALPHA = 0.5
PITCH_ANGLE = 2.0 * math.pi / 36.0
NYQUIST_DAMP = 2.0
Y_PARTS = 2


def extended_2(block, sides, width):
    for axis, dim in sides:
        count = lax.axis_size(axis)
        forward = [(i, i + 1) for i in range(count - 1)]
        backward = [(target, source) for source, target in forward]
        low = lax.ppermute(
            lax.slice_in_dim(block, block.shape[dim] - width, None, axis=dim), axis, forward
        )
        high = lax.ppermute(lax.slice_in_dim(block, 0, width, axis=dim), axis, backward)
        block = jnp.concatenate([low, block, high], axis=dim)
    return block


def time_weights(offset, count):
    offset = offset % count
    angle = math.pi * offset.astype(jnp.float32) / count
    parity = jnp.where(offset % 2 == 1, 1.0, -1.0).astype(jnp.float32)
    sine = jnp.where(offset == 0, 1.0, jnp.sin(angle))
    spectral = 0.5 * parity * jnp.cos(angle) / sine - NYQUIST_DAMP * parity / count
    return jnp.where(offset == 0, NYQUIST_DAMP / count, spectral)


def rotate_velocity(values, turn):
    cosine = math.cos(PITCH_ANGLE)
    sine = turn * math.sin(PITCH_ANGLE)
    second = values[:, 2]
    third = values[:, 3]
    return jnp.stack(
        [
            values[:, 0],
            values[:, 1],
            cosine * second - sine * third,
            sine * second + cosine * third,
            values[:, 4],
        ],
        axis=1,
    )


def section_spatial(state, eddy_visc, jacobians, up_i, down_i, low_ghost, high_ghost):
    up_j = jnp.concatenate([state[:, :, :, 1:], high_ghost[:, :, :, None]], axis=3)
    down_j = jnp.concatenate([low_ghost[:, :, :, None], state[:, :, :, :-1]], axis=3)
    zeros = jnp.zeros(state.shape[:4] + (1,), state.dtype)
    up_k = jnp.concatenate([state[..., 1:], zeros], axis=4)
    down_k = jnp.concatenate([zeros, state[..., :-1]], axis=4)
    diffs = [(up_i - down_i) * 0.5, (up_j - down_j) * 0.5, (up_k - down_k) * 0.5]
    flux = None
    for direction, diff in enumerate(diffs):
        for source in range(state.shape[1]):
            column = jacobians[direction, :, source].reshape((1, -1) + (1,) * (state.ndim - 2))
            term = column * diff[:, source : source + 1]
            flux = term if flux is None else flux + term
    laplace = up_i + down_i + up_j + down_j + up_k + down_k - 6.0 * state
    return flux - eddy_visc[None, None] * laplace


def per_device(state, base, pseudo_step, eddy_visc, jacobians, partner_radial, partner_instance):
    ring = lax.axis_size("tz")
    total_count = ring * Y_PARTS
    z = lax.axis_index("tz")
    y = lax.axis_index("ty")
    own = Y_PARTS * z + y
    partner = own + 1 - 2 * y
    swap = [(i, Y_PARTS - 1 - i) for i in range(Y_PARTS)]
    ring_ids = Y_PARTS * jnp.arange(ring, dtype=jnp.int32) + y
    pitch = state.shape[3]
    edge = pitch // 4
    inner = state[:, :, :, edge : pitch - edge]
    other = lax.ppermute(inner, "ty", swap)
    expand = (ring,) + (1,) * (inner.ndim - 1)
    own_weights = time_weights(ring_ids - own, total_count).reshape(expand)
    partner_weights = time_weights(ring_ids - partner, total_count).reshape(expand)
    contributions = own_weights * inner + partner_weights * other
    inner_term = lax.psum_scatter(contributions, "tz", scatter_dimension=0, tiled=True)
    outer = jnp.concatenate([state[:, :, :, :edge], state[:, :, :, pitch - edge :]], axis=3)
    held = lax.all_gather(outer, "tz", axis=0, tiled=True)
    targets = jnp.stack([own, partner])
    weights = time_weights(targets[:, None] - ring_ids[None, :], total_count)
    partial = jnp.sum(weights.reshape((2, ring) + (1,) * (held.ndim - 1)) * held[None], axis=1)
    faces = jnp.stack([held[:, :, :, -1, :], held[:, :, :, 0, :]], axis=0)
    radial_count = partner_radial.shape[2]
    radial_hot = (partner_radial[..., None] == jnp.arange(radial_count, dtype=jnp.int32)).astype(
        jnp.float32
    )
    remapped = jnp.einsum("szvir,sikr->szvik", faces, radial_hot, precision=lax.Precision.HIGHEST)
    shifts = (targets - own)[:, None, None, None]
    sources = (partner_instance[0][None] + shifts) % total_count
    instance_hot = (sources[..., None] == ring_ids).astype(jnp.float32)
    picked = jnp.sum(instance_hot[:, :, None] * jnp.moveaxis(remapped, 1, -1)[None], axis=-1)
    message = jnp.concatenate([partial[1].reshape(-1), picked[1].reshape(-1)])
    received = lax.ppermute(message, "ty", swap)
    split = partial[0].size
    outer_term = partial[:1] + received[:split].reshape((1,) + partial.shape[1:])
    ghosts = picked[0] + received[split:].reshape(picked.shape[1:])
    time_term = jnp.concatenate(
        [outer_term[:, :, :, :edge], inner_term, outer_term[:, :, :, edge:]], axis=3
    )
    low_ghost = rotate_velocity(ghosts[0][None], -1.0)
    high_ghost = rotate_velocity(ghosts[1][None], 1.0)
    extended = extended_2(state, (("space", 2),), 1)
    up_i = extended[:, :, 2:]
    down_i = extended[:, :, :-2]
    spatial = lax.optimization_barrier(
        section_spatial(state, eddy_visc, jacobians, up_i, down_i, low_ghost, high_ghost)
    )
    return base - SECTION_ALPHA * pseudo_step[None, None] * (spatial + time_term)


def solution(mesh):
    devices = mesh.devices
    cells = devices.shape[1]
    split_mesh = Mesh(
        devices.reshape(devices.shape[0] // Y_PARTS, Y_PARTS, cells), ("tz", "ty", "space")
    )
    time_axes = ("tz", "ty")
    return jax.shard_map(
        per_device,
        mesh=split_mesh,
        in_specs=(
            P(time_axes, None, "space", None, None),
            P(time_axes, None, "space", None, None),
            P("space", None, None),
            P("space", None, None),
            P(),
            P(None, "space", None),
            P(time_axes, None, "space", None),
        ),
        out_specs=P(time_axes, None, "space", None, None),
        check_vma=False,
    )
```

profile of v0, /device:TPU:2, one launch (start us, length us, event | category | flops | bytes accessed | tf_op | source)
XLA Modules:
  0.0 117.2 jit_solution(7916101641822765204)
XLA Ops:
  6.5 0.0 all-gather.2.cloned.1.call-start
  6.5 1.1 fusion.22
  7.6 0.7 pad_maximum_fusion.5
  8.4 0.0 all-gather.2.cloned.1.call-update
  8.4 0.0 reduce-scatter.2.cloned.1.call-start
  8.5 1.6 %fusion.20 = (f32[1,5,1,32,128]{4,3,2,1,0:T(8,128)}, f32[1,5,1,32,128]{4,3,2,1,0:T(8,128)}) fusion(f32[1,5,8,32,128]{4,3,2,1,0:T(8,128)} %param.7), kind=kLoop, calls=%fused_computation.113 | loop fusion | bytes 327680 | tf_op jit(solution)/shard_map/slice | solution.py:20
  10.1 4.9 %collective-permute-start = (f32[1,5,1,32,128]{4,3,2,1,0:T(8,128)}, f32[1,5,1,32,128]{4,3,2,1,0:T(8,128)}, u32[]{:S(2)}, u32[]{:S(2)}) collective-permute-start(f32[1,5,1,32,128]{4,3,2,1,0:T(8,128)} %get-tuple-element.42), channel_id=1, source_target_pairs={{1,0},{2,1},{3,2},{4,3},{5,4},{6,5},{7,6},{8,7},{9,8},{10,9},{11,1... | collective-permute-start | bytes 245768 | tf_op jit(solution)/shard_map/ppermute | solution.py:22
  15.0 0.0 copy-start.11
  15.0 1.9 %collective-permute-start.1 = (f32[1,5,1,32,128]{4,3,2,1,0:T(8,128)}, f32[1,5,1,32,128]{4,3,2,1,0:T(8,128)}, u32[]{:S(2)}, u32[]{:S(2)}) collective-permute-start(f32[1,5,1,32,128]{4,3,2,1,0:T(8,128)} %get-tuple-element.41), channel_id=1, source_target_pairs={{0,1},{1,2},{2,3},{3,4},{4,5},{5,6},{6,7},{7,8},{8,9},{9,10},{10,1... | collective-permute-start | bytes 245768 | tf_op jit(solution)/shard_map/ppermute | solution.py:19
  16.9 1.9 %slice_bitcast_fusion.16 = (f32[5,8,16,128]{3,2,1,0:T(8,128)}, f32[1,5,8,16,128]{4,3,2,1,0:T(8,128)}) fusion(f32[1,5,8,32,128]{4,3,2,1,0:T(8,128)} %param.7), kind=kLoop, calls=%fused_computation.111 | loop fusion | bytes 983040 | tf_op jit(solution)/shard_map/mul | solution.py:86
  18.8 5.3 %collective-permute-start.3 = (f32[1,5,8,16,128]{4,3,2,1,0:T(8,128)}, f32[1,5,8,16,128]{4,3,2,1,0:T(8,128)}, u32[]{:S(2)}, u32[]{:S(2)}) collective-permute-start(f32[1,5,8,16,128]{4,3,2,1,0:T(8,128)} %get-tuple-element.25), channel_id=1, source_target_pairs={{0,32},{32,0},{1,33},{33,1},{2,34},{34,2},{3,35},{35,3},{4,36},{36... | collective-permute-start | bytes 983048 | tf_op jit(solution)/shard_map/ppermute | solution.py:82
  24.2 0.1 broadcast_subtract_fusion
  24.2 0.0 copy-done
  24.2 0.2 fusion.23
  24.5 1.1 subtract_multiply_fusion
  25.6 0.1 subtract_select_fusion
  25.7 0.0 copy-done.11
  25.7 0.1 add_select_fusion.1
  25.8 0.7 compare_convert_fusion
  26.5 0.0 copy-done.10
  26.5 0.7 broadcast_multiply_fusion
  27.2 0.1 compare_select_fusion.15
  27.3 0.1 fusion.21
  27.4 7.7 %collective-permute-done.3 = f32[1,5,8,16,128]{4,3,2,1,0:T(8,128)} collective-permute-done((f32[1,5,8,16,128]{4,3,2,1,0:T(8,128)}, f32[1,5,8,16,128]{4,3,2,1,0:T(8,128)}, u32[]{:S(2)}, u32[]{:S(2)}) %collective-permute-start.3) | collective-permute-done | bytes 327712 | tf_op jit(solution)/shard_map/ppermute | solution.py:82
  35.1 0.0 copy-done.3
  35.1 2.9 %multiply_add_fusion = f32[8,5,8,16,128]{4,3,2,1,0:T(8,128)} fusion(f32[5,8,16,128]{3,2,1,0:T(8,128)} %bitcast.33, f32[8]{0:T(128)S(1)} %get-tuple-element.61, f32[5,8,16,128]{3,2,1,0:T(8,128)S(1)} %copy-done.3, f32[8]{0:T(128)S(1)} %get-tuple-element.62), kind=kLoop, calls=%fused_computation.1 | loop fusion | flops 1966080 | bytes 3276864 | tf_op jit(solution)/shard_map/add | solution.py:86
  38.0 0.0 reduce-scatter.2.cloned.1.call-update
  38.1 0.0 copy-done.8
  38.1 0.9 slice_reduce_fusion.14
  39.0 1.9 %slice_bitcast_fusion.4 = (f32[8,32,128]{2,1,0:T(8,128)S(1)}, f32[8,32,128]{2,1,0:T(8,128)S(1)}, f32[8,32,128]{2,1,0:T(8,128)}, f32[8,32,128]{2,1,0:T(8,128)}, f32[8,32,128]{2,1,0:T(8,128)}) fusion(f32[1,5,8,32,128]{4,3,2,1,0:T(8,128)} %subtract_multiply_fusion), kind=kLoop, calls=%fused_computation.30 | loop fusion | bytes 1310720 | tf_op jit(solution)/shard_map/mul | solution.py:64
  40.9 19.1 %all-gather.2.cloned.1.call-done = f32[8,5,8,16,128]{4,3,2,1,0:T(8,128)} async-done(((f32[1,5,8,16,128]{4,3,2,1,0:T(8,128)}), f32[8,5,8,16,128]{4,3,2,1,0:T(8,128)}) %all-gather.2.cloned.1.call-update) | async-done | bytes 2621456 | tf_op jit(solution)/shard_map/all_gather | solution.py:89
  60.0 2.2 %fusion.19 = (f32[8,5,8,1,128]{4,3,2,1,0:T(1,128)S(1)}, f32[8,5,8,1,128]{4,3,2,1,0:T(1,128)S(1)}) fusion(f32[8,5,8,16,128]{4,3,2,1,0:T(8,128)} %all-gather.2.cloned.1.call-done), kind=kLoop, calls=%fused_computation.112 | loop fusion | bytes 655360 | tf_op jit(solution)/shard_map/slice | solution.py:93
  62.1 0.1 copy_bitcast_fusion
  62.2 2.1 %convolution_bitcast_fusion = f32[2,5,8,128,8]{3,4,1,2,0:T(8,128)S(1)} fusion(s32[2,8,128]{2,1,0:T(8,128)} %param.12, f32[1,8,5,8,128]{4,1,2,3,0:T(8,128)S(1)} %get-tuple-element.59, f32[1,8,5,8,128]{4,1,2,3,0:T(8,128)S(1)} %get-tuple-element.60), kind=kOutput, calls=%fused_computation.2 | convolution fusion | flops 126173184 | bytes 663552 | tf_op jit(solution)/shard_map/szvir,sikr->szvik/dot_general | solution.py:98
  64.4 1.1 multiply_reduce_fusion.1
  65.5 0.4 multiply_reduce_fusion
  66.0 7.1 %collective-permute-start.2 = (f32[92160]{0:T(1024)S(1)}, f32[92160]{0:T(1024)S(1)}, u32[]{:S(2)}, u32[]{:S(2)}) collective-permute-start(f32[92160]{0:T(1024)S(1)} %pad_maximum_fusion.4), channel_id=1, source_target_pairs={{0,32},{32,0},{1,33},{33,1},{2,34},{34,2},{3,35},{35,3},{4,36},{36... | collective-permute-start | bytes 1105928 | tf_op jit(solution)/shard_map/ppermute | solution.py:104
  73.1 0.0 collective-permute-done
  73.1 0.0 collective-permute-done.1
  73.1 1.0 subtract_multiply_fusion.2
  74.1 0.0 copy-start.9
  74.3 0.1 slice_bitcast_fusion.14
  74.3 8.3 %collective-permute-done.2 = f32[92160]{0:T(1024)S(1)} collective-permute-done((f32[92160]{0:T(1024)S(1)}, f32[92160]{0:T(1024)S(1)}, u32[]{:S(2)}, u32[]{:S(2)}) %collective-permute-start.2) | collective-permute-done | bytes 368672 | tf_op jit(solution)/shard_map/ppermute | solution.py:104
  82.7 0.2 subtract_multiply_fusion.1
  82.9 0.1 slice_bitcast_fusion.9
  83.1 3.0 %multiply_subtract_fusion = f32[1,5,8,32,128]{4,3,2,1,0:T(8,128)} fusion(f32[1,5,8,32,128]{4,3,2,1,0:T(8,128)S(1)} %copy-done, f32[1,5,8,32,127]{4,3,2,1,0:T(8,128)S(1)} %get-tuple-element.48, f32[1,5,8,32,127]{4,3,2,1,0:T(8,128)S(1)} %get-tuple-element.47, f32[1,5,8,31,128]{4,3,2,1,0:T(8,128)S(1)} %get-tuple-element.44, ...), kind=kLoop, calls=%fused_computation.12 | loop fusion | flops 6881280 | bytes 6183212 | tf_op jit(solution)/shard_map/sub | solution.py:67
  86.2 22.1 %reduce-scatter.2.cloned.1.call-done = f32[1,5,8,16,128]{4,3,2,1,0:T(8,128)} async-done(((f32[8,5,8,16,128]{4,3,2,1,0:T(8,128)}), f32[1,5,8,16,128]{4,3,2,1,0:T(8,128)}) %reduce-scatter.2.cloned.1.call-update) | async-done | bytes 327696 | tf_op jit(solution)/shard_map/reduce_scatter | solution.py:87
  108.4 2.0 %fusion.3 = f32[1,5,8,32,128]{4,3,2,1,0:T(8,128)} fusion(f32[1,5,8,32,128]{4,3,2,1,0:T(8,128)S(1)} %copy-done.4, f32[1,5,8,32,128]{4,3,2,1,0:T(8,128)S(1)} %copy-done.2, f32[1,5,8,8,128]{4,3,2,1,0:T(8,128)S(1)} %get-tuple-element.50, f32[1,5,8,16,128]{4,3,2,1,0:T(8,128)} %reduce-scatter.2.cloned.1.call-done, f32[1,5,8,8,128]{4,3,2,1,0:T(8,128)S(1)} %get-tuple-element.49, ...), kind=kLoop, calls=%fused_computation.11 | loop fusion | flops 819200 | bytes 2752512 | tf_op jit(solution)/shard_map/sub | solution.py:119
  (54 shorter events, 0.3 us)
Async XLA Ops:
  6.5 17.7 %copy-start = (f32[1,5,8,32,128]{4,3,2,1,0:T(8,128)S(1)}, f32[1,5,8,32,128]{4,3,2,1,0:T(8,128)}, u32[]{:S(2)}) copy-start(f32[1,5,8,32,128]{4,3,2,1,0:T(8,128)} %param.7) | copy-start | bytes 1966084
  6.5 53.4 %all-gather.2.cloned.1.call-start = ((), (), s32[]{:S(2)}) async-start(), calls=%async_computation.1 | async-start | bytes 2949120 | tf_op jit(solution)/shard_map/all_gather | solution.py:89
  8.4 100.0 %reduce-scatter.2.cloned.1.call-start = ((), (), s32[]{:S(2)}) async-start(), calls=%async_computation.2 | async-start | bytes 2949120 | tf_op jit(solution)/shard_map/reduce_scatter | solution.py:87
  10.1 63.0 %collective-permute-start = (f32[1,5,1,32,128]{4,3,2,1,0:T(8,128)}, f32[1,5,1,32,128]{4,3,2,1,0:T(8,128)}, u32[]{:S(2)}, u32[]{:S(2)}) collective-permute-start(f32[1,5,1,32,128]{4,3,2,1,0:T(8,128)} %get-tuple-element.42), channel_id=1, source_target_pairs={{1,0},{2,1},{3,2},{4,3},{5,4},{6,5},{7,6},{8,7},{9,8},{10,9},{11,1... | collective-permute-start | bytes 245768 | tf_op jit(solution)/shard_map/ppermute | solution.py:22
  15.0 10.7 %copy-start.11 = (s32[1,2,8,128]{3,2,1,0:T(8,128)S(1)}, s32[1,2,8,128]{3,2,1,0:T(8,128)}, u32[]{:S(2)}) copy-start(s32[1,2,8,128]{3,2,1,0:T(8,128)} %param.13) | copy-start | bytes 24580
  15.0 58.1 %collective-permute-start.1 = (f32[1,5,1,32,128]{4,3,2,1,0:T(8,128)}, f32[1,5,1,32,128]{4,3,2,1,0:T(8,128)}, u32[]{:S(2)}, u32[]{:S(2)}) collective-permute-start(f32[1,5,1,32,128]{4,3,2,1,0:T(8,128)} %get-tuple-element.41), channel_id=1, source_target_pairs={{0,1},{1,2},{2,3},{3,4},{4,5},{5,6},{6,7},{7,8},{8,9},{9,10},{10,1... | collective-permute-start | bytes 245768 | tf_op jit(solution)/shard_map/ppermute | solution.py:19
  18.8 7.7 %copy-start.10 = (f32[8,32,128]{2,1,0:T(8,128)S(1)}, f32[8,32,128]{2,1,0:T(8,128)}, u32[]{:S(2)}) copy-start(f32[8,32,128]{2,1,0:T(8,128)} %param.9) | copy-start | bytes 393220
  18.8 16.3 %collective-permute-start.3 = (f32[1,5,8,16,128]{4,3,2,1,0:T(8,128)}, f32[1,5,8,16,128]{4,3,2,1,0:T(8,128)}, u32[]{:S(2)}, u32[]{:S(2)}) collective-permute-start(f32[1,5,8,16,128]{4,3,2,1,0:T(8,128)} %get-tuple-element.25), channel_id=1, source_target_pairs={{0,32},{32,0},{1,33},{33,1},{2,34},{34,2},{3,35},{35,3},{4,36},{36... | collective-permute-start | bytes 983048 | tf_op jit(solution)/shard_map/ppermute | solution.py:82
  24.5 10.6 %copy-start.3 = (f32[5,8,16,128]{3,2,1,0:T(8,128)S(1)}, f32[5,8,16,128]{3,2,1,0:T(8,128)}, u32[]{:S(2)}) copy-start(f32[5,8,16,128]{3,2,1,0:T(8,128)} %get-tuple-element.24) | copy-start | bytes 983044
  35.1 3.0 %copy-start.8 = (f32[3,5,5]{2,0,1:T(4,128)S(1)}, f32[3,5,5]{2,0,1:T(4,128)}, u32[]{:S(2)}) copy-start(f32[3,5,5]{2,0,1:T(4,128)} %param.11) | copy-start | bytes 904
  60.0 5.5 %copy-start.1 = (f32[8,5,8,16,128]{4,3,2,1,0:T(8,128)S(1)}, f32[8,5,8,16,128]{4,3,2,1,0:T(8,128)}, u32[]{:S(2)}) copy-start(f32[8,5,8,16,128]{4,3,2,1,0:T(8,128)} %all-gather.2.cloned.1.call-done) | copy-start | bytes 7864324
  66.0 16.7 %collective-permute-start.2 = (f32[92160]{0:T(1024)S(1)}, f32[92160]{0:T(1024)S(1)}, u32[]{:S(2)}, u32[]{:S(2)}) collective-permute-start(f32[92160]{0:T(1024)S(1)} %pad_maximum_fusion.4), channel_id=1, source_target_pairs={{0,32},{32,0},{1,33},{33,1},{2,34},{34,2},{3,35},{35,3},{4,36},{36... | collective-permute-start | bytes 1105928 | tf_op jit(solution)/shard_map/ppermute | solution.py:104
  74.1 8.9 %copy-start.5 = (f32[8,32,128]{2,1,0:T(8,128)S(1)}, f32[8,32,128]{2,1,0:T(8,128)}, u32[]{:S(2)}) copy-start(f32[8,32,128]{2,1,0:T(8,128)} %get-tuple-element.38) | copy-start | bytes 393220
  74.1 8.9 %copy-start.6 = (f32[8,32,128]{2,1,0:T(8,128)S(1)}, f32[8,32,128]{2,1,0:T(8,128)}, u32[]{:S(2)}) copy-start(f32[8,32,128]{2,1,0:T(8,128)} %get-tuple-element.39) | copy-start | bytes 393220
  74.1 8.9 %copy-start.7 = (f32[8,32,128]{2,1,0:T(8,128)S(1)}, f32[8,32,128]{2,1,0:T(8,128)}, u32[]{:S(2)}) copy-start(f32[8,32,128]{2,1,0:T(8,128)} %get-tuple-element.40) | copy-start | bytes 393220
  74.1 8.9 %copy-start.9 = (f32[8,32,128]{2,1,0:T(8,128)S(1)}, f32[8,32,128]{2,1,0:T(8,128)}, u32[]{:S(2)}) copy-start(f32[8,32,128]{2,1,0:T(8,128)} %param.10) | copy-start | bytes 393220
  74.1 8.9 %copy-start.12 = (f32[5]{0:T(128)S(1)}, f32[5]{0:T(128)}, u32[]{:S(2)}) copy-start(f32[5]{0:T(128)} %get-tuple-element.8) | copy-start | bytes 64
  74.2 8.9 %copy-start.13 = (f32[5]{0:T(128)S(1)}, f32[5]{0:T(128)}, u32[]{:S(2)}) copy-start(f32[5]{0:T(128)} %get-tuple-element.9) | copy-start | bytes 64
  74.2 8.9 %copy-start.14 = (f32[5]{0:T(128)S(1)}, f32[5]{0:T(128)}, u32[]{:S(2)}) copy-start(f32[5]{0:T(128)} %get-tuple-element.10) | copy-start | bytes 64
  74.2 8.9 %copy-start.15 = (f32[5]{0:T(128)S(1)}, f32[5]{0:T(128)}, u32[]{:S(2)}) copy-start(f32[5]{0:T(128)} %get-tuple-element.11) | copy-start | bytes 64
  74.2 8.9 %copy-start.16 = (f32[5]{0:T(128)S(1)}, f32[5]{0:T(128)}, u32[]{:S(2)}) copy-start(f32[5]{0:T(128)} %get-tuple-element.12) | copy-start | bytes 64
  74.2 8.9 %copy-start.17 = (f32[5]{0:T(128)S(1)}, f32[5]{0:T(128)}, u32[]{:S(2)}) copy-start(f32[5]{0:T(128)} %get-tuple-element.13) | copy-start | bytes 64
  74.2 8.9 %copy-start.18 = (f32[5]{0:T(128)S(1)}, f32[5]{0:T(128)}, u32[]{:S(2)}) copy-start(f32[5]{0:T(128)} %get-tuple-element.14) | copy-start | bytes 64
  74.2 8.9 %copy-start.19 = (f32[5]{0:T(128)S(1)}, f32[5]{0:T(128)}, u32[]{:S(2)}) copy-start(f32[5]{0:T(128)} %get-tuple-element.15) | copy-start | bytes 64
  74.2 8.9 %copy-start.20 = (f32[5]{0:T(128)S(1)}, f32[5]{0:T(128)}, u32[]{:S(2)}) copy-start(f32[5]{0:T(128)} %get-tuple-element.16) | copy-start | bytes 64
  74.2 8.9 %copy-start.21 = (f32[5]{0:T(128)S(1)}, f32[5]{0:T(128)}, u32[]{:S(2)}) copy-start(f32[5]{0:T(128)} %get-tuple-element.17) | copy-start | bytes 64
  74.2 8.9 %copy-start.22 = (f32[5]{0:T(128)S(1)}, f32[5]{0:T(128)}, u32[]{:S(2)}) copy-start(f32[5]{0:T(128)} %get-tuple-element.18) | copy-start | bytes 64
  74.3 8.9 %copy-start.23 = (f32[5]{0:T(128)S(1)}, f32[5]{0:T(128)}, u32[]{:S(2)}) copy-start(f32[5]{0:T(128)} %get-tuple-element.19) | copy-start | bytes 64
  86.1 22.3 %copy-start.2 = (f32[1,5,8,32,128]{4,3,2,1,0:T(8,128)S(1)}, f32[1,5,8,32,128]{4,3,2,1,0:T(8,128)}, u32[]{:S(2)}) copy-start(f32[1,5,8,32,128]{4,3,2,1,0:T(8,128)} %multiply_subtract_fusion) | copy-start | bytes 1966084
  86.1 22.3 %copy-start.4 = (f32[1,5,8,32,128]{4,3,2,1,0:T(8,128)S(1)}, f32[1,5,8,32,128]{4,3,2,1,0:T(8,128)}, u32[]{:S(2)}) copy-start(f32[1,5,8,32,128]{4,3,2,1,0:T(8,128)} %param.8) | copy-start | bytes 1966084
Sparse Core Ops, SparseCore 0:
  9.4 50.4 all-gather.1
  62.8 45.4 reduce-scatter.1
where the time goes:
time: 118 us; the launch traced here: 117 us
  waiting for transfers between devices  57.3 us (49%)
  starting transfers between devices  19.3 us (16%)
  other arithmetic  14.4 us (12%)
  between operations  13.9 us (12%)
  local copies, waits for them, and re-layouts  10.3 us (9%)
  matrix products  2.13 us (2%)
    reduce_scatter x1, waiting for transfers between devices, per_device(): lax.psum_scatter(contributions, 'tz', scatter_dimension=0, tiled=True)  22.1 us
    all_gather x1, waiting for transfers between devices, per_device(): held = lax.all_gather(outer, 'tz', axis=0, tiled=True)  19.1 us
    ppermute x1, waiting for transfers between devices, per_device(): received = lax.ppermute(message, 'ty', swap)  8.32 us
    ppermute x1, waiting for transfers between devices, per_device(): other = lax.ppermute(inner, 'ty', swap)  7.71 us
    ppermute x1, starting transfers between devices, per_device(): received = lax.ppermute(message, 'ty', swap)  7.05 us
    ppermute x1, starting transfers between devices, per_device(): other = lax.ppermute(inner, 'ty', swap)  5.34 us
    ppermute x1, starting transfers between devices, extended_2(): lax.ppermute(lax.slice_in_dim(block, 0, width, axis=dim), axis, backward)  4.91 us
    sub x1, other arithmetic, section_spatial(): return flux - eddy_visc[None, None] * laplace  2.97 us
  transfers between devices with their start and end apart: 6, of which 4 were waited for; matrix products, arithmetic and copies ran while one was open for 19% of the time, Pallas kernels for 0%

commit v1 on v0

--- a/solution.py
+++ b/solution.py
@@ -86,7 +86,9 @@
     contributions = own_weights * inner + partner_weights * other
     inner_term = lax.psum_scatter(contributions, "tz", scatter_dimension=0, tiled=True)
     outer = jnp.concatenate([state[:, :, :, :edge], state[:, :, :, pitch - edge :]], axis=3)
-    held = lax.all_gather(outer, "tz", axis=0, tiled=True)
+    held = jnp.concatenate(
+        lax.all_to_all(jnp.stack([outer] * lax.axis_size("tz")), "tz", 0, 0), axis=0
+    )
     targets = jnp.stack([own, partner])
     weights = time_weights(targets[:, None] - ring_ids[None, :], total_count)
     partial = jnp.sum(weights.reshape((2, ring) + (1,) * (held.ndim - 1)) * held[None], axis=1)

time: 118 us -> 126 us (1.068)
  the two profiles are of different devices: /device:TPU:2 before, /device:TPU:63 now
where the time goes in v1:
time: 126 us
  waiting for transfers between devices  61.8 us (49%)
  starting transfers between devices  24.1 us (19%)
  between operations  14 us (11%)
  local copies, waits for them, and re-layouts  12.3 us (10%)
  other arithmetic  11.8 us (9%)
  matrix products  1.43 us (1%)
    all_to_all x1, waiting for transfers between devices, per_device(): lax.all_to_all(jnp.stack([outer] * lax.axis_size('tz')), 'tz', 0, 0)  34.3 us
    ppermute x1, waiting for transfers between devices, per_device(): received = lax.ppermute(message, 'ty', swap)  18.6 us
    all_to_all x1, starting transfers between devices, per_device(): lax.all_to_all(jnp.stack([outer] * lax.axis_size('tz')), 'tz', 0, 0)  10.2 us
    ppermute x1, waiting for transfers between devices, per_device(): other = lax.ppermute(inner, 'ty', swap)  8.84 us
    ppermute x1, starting transfers between devices, per_device(): other = lax.ppermute(inner, 'ty', swap)  4.55 us
    ppermute x1, starting transfers between devices, per_device(): received = lax.ppermute(message, 'ty', swap)  4.45 us
    ppermute x1, starting transfers between devices, extended_2(): lax.ppermute(lax.slice_in_dim(block, 0, width, axis=dim), axis, backward)  3.49 us
    add x1, other arithmetic, per_device(): contributions = own_weights * inner + partner_weights * other  2.93 us
  transfers between devices with their start and end apart: 6, of which 3 were waited for; matrix products, arithmetic and copies ran while one was open for 15% of the time, Pallas kernels for 0%

profile of v1, /device:TPU:63, one launch (start us, length us, event | category | flops | bytes accessed | tf_op | source)
XLA Modules:
  0.0 125.5 jit_solution(15364141194878022095)
XLA Ops:
  6.5 1.0 fusion.21
  7.6 1.8 %stack.38 = f32[8,1,5,8,16,128]{5,4,3,2,1,0:T(8,128)} broadcast(f32[5,8,16,128]{3,2,1,0:T(8,128)S(1)} %maximum_bitcast_fusion), dimensions={2,3,4,5} | broadcast | bytes 2949120 | tf_op jit(solution)/shard_map/stack | solution.py:90
  9.4 10.2 %all-to-all-start = ((f32[8,1,5,8,16,128]{5,4,3,2,1,0:T(8,128)}), f32[8,1,5,8,16,128]{5,4,3,2,1,0:T(8,128)S(1)}, u32[]{:S(2)}, u32[]{:S(2)}) async-start(f32[8,1,5,8,16,128]{5,4,3,2,1,0:T(8,128)} %stack.38), calls=%async_computation | async-start | bytes 5242880 | tf_op jit(solution)/shard_map/all_to_all | solution.py:90
  19.6 0.0 reduce-scatter.2.cloned.1.call-start
  19.6 0.7 fusion.19
  20.3 3.5 %collective-permute-start = (f32[1,5,1,32,128]{4,3,2,1,0:T(8,128)}, f32[1,5,1,32,128]{4,3,2,1,0:T(8,128)}, u32[]{:S(2)}, u32[]{:S(2)}) collective-permute-start(f32[1,5,1,32,128]{4,3,2,1,0:T(8,128)} %get-tuple-element.42), channel_id=1, source_target_pairs={{1,0},{2,1},{3,2},{4,3},{5,4},{6,5},{7,6},{8,7},{9,8},{10,9},{11,1... | collective-permute-start | bytes 245768 | tf_op jit(solution)/shard_map/ppermute | solution.py:22
  23.8 1.4 %collective-permute-start.1 = (f32[1,5,1,32,128]{4,3,2,1,0:T(8,128)}, f32[1,5,1,32,128]{4,3,2,1,0:T(8,128)}, u32[]{:S(2)}, u32[]{:S(2)}) collective-permute-start(f32[1,5,1,32,128]{4,3,2,1,0:T(8,128)} %get-tuple-element.41), channel_id=1, source_target_pairs={{0,1},{1,2},{2,3},{3,4},{4,5},{5,6},{6,7},{7,8},{8,9},{9,10},{10,1... | collective-permute-start | bytes 245768 | tf_op jit(solution)/shard_map/ppermute | solution.py:19
  25.2 0.9 slice_bitcast_fusion.18
  26.1 4.6 %collective-permute-start.3 = (f32[1,5,8,16,128]{4,3,2,1,0:T(8,128)}, f32[1,5,8,16,128]{4,3,2,1,0:T(8,128)}, u32[]{:S(2)}, u32[]{:S(2)}) collective-permute-start(f32[1,5,8,16,128]{4,3,2,1,0:T(8,128)} %get-tuple-element.25), channel_id=1, source_target_pairs={{0,32},{32,0},{1,33},{33,1},{2,34},{34,2},{3,35},{35,3},{4,36},{36... | collective-permute-start | bytes 983048 | tf_op jit(solution)/shard_map/ppermute | solution.py:82
  30.7 0.1 broadcast_subtract_fusion
  30.8 0.2 fusion.22
  31.1 0.0 copy-start.5
  31.1 0.9 copy-done.3
  31.9 1.1 subtract_multiply_fusion
  33.1 0.1 subtract_select_fusion
  33.2 0.0 copy-done.17
  33.2 0.1 add_select_fusion.1
  33.3 0.7 compare_convert_fusion
  34.0 0.1 compare_select_fusion.15
  34.1 0.7 broadcast_multiply_fusion
  34.7 8.8 %collective-permute-done.3 = f32[1,5,8,16,128]{4,3,2,1,0:T(8,128)} collective-permute-done((f32[1,5,8,16,128]{4,3,2,1,0:T(8,128)}, f32[1,5,8,16,128]{4,3,2,1,0:T(8,128)}, u32[]{:S(2)}, u32[]{:S(2)}) %collective-permute-start.3) | collective-permute-done | bytes 327712 | tf_op jit(solution)/shard_map/ppermute | solution.py:82
  43.6 0.0 copy-done.7
  43.6 2.9 %multiply_add_fusion = f32[8,5,8,16,128]{4,3,2,1,0:T(8,128)} fusion(f32[5,8,16,128]{3,2,1,0:T(8,128)} %bitcast.36, f32[8]{0:T(128)S(1)} %get-tuple-element.59, f32[5,8,16,128]{3,2,1,0:T(8,128)S(1)} %copy-done.7, f32[8]{0:T(128)S(1)} %get-tuple-element.60), kind=kLoop, calls=%fused_computation.2 | loop fusion | flops 1966080 | bytes 3276864 | tf_op jit(solution)/shard_map/add | solution.py:86
  46.5 0.0 reduce-scatter.2.cloned.1.call-update
  46.6 0.9 slice_reduce_fusion.14
  47.4 1.9 %slice_bitcast_fusion.6 = (f32[8,32,128]{2,1,0:T(8,128)S(1)}, f32[8,32,128]{2,1,0:T(8,128)S(1)}, f32[8,32,128]{2,1,0:T(8,128)}, f32[8,32,128]{2,1,0:T(8,128)}, f32[8,32,128]{2,1,0:T(8,128)}) fusion(f32[1,5,8,32,128]{4,3,2,1,0:T(8,128)} %subtract_multiply_fusion), kind=kLoop, calls=%fused_computation.31 | loop fusion | bytes 1310720 | tf_op jit(solution)/shard_map/mul | solution.py:64
  49.4 1.2 fusion.20
  50.5 34.3 %all-to-all-done = f32[8,1,5,8,16,128]{5,4,3,2,1,0:T(8,128)S(1)} async-done(((f32[8,1,5,8,16,128]{5,4,3,2,1,0:T(8,128)}), f32[8,1,5,8,16,128]{5,4,3,2,1,0:T(8,128)S(1)}, u32[]{:S(2)}, u32[]{:S(2)}) %all-to-all-start) | async-done | bytes 2621472 | tf_op jit(solution)/shard_map/all_to_all | solution.py:90
  84.9 1.5 %copy.35 = f32[8,1,5,8,16,128]{5,0,2,3,4,1:T(8,128)S(1)} copy(f32[8,1,5,8,16,128]{5,4,3,2,1,0:T(8,128)S(1)} %all-to-all-done) | data formatting | bytes 5242880 | tf_op jit(solution)/shard_map/all_to_all | solution.py:90
  86.4 1.4 %convolution_bitcast_fusion = f32[2,5,8,128,8]{3,4,1,2,0:T(8,128)S(1)} fusion(s32[2,8,128]{2,1,0:T(8,128)S(1)} %copy-done.30, f32[1,8,5,8,128]{4,1,2,3,0:T(8,128)S(1)} %get-tuple-element.23, f32[1,8,5,8,128]{4,1,2,3,0:T(8,128)S(1)} %get-tuple-element.22), kind=kOutput, calls=%fused_computation.3 | convolution fusion | flops 126173184 | bytes 663552 | tf_op jit(solution)/shard_map/szvir,sikr->szvik/dot_general | solution.py:100
  87.9 0.2 multiply_reduce_fusion.1
  88.1 0.4 multiply_reduce_fusion
  88.6 4.4 %collective-permute-start.2 = (f32[92160]{0:T(1024)S(1)}, f32[92160]{0:T(1024)S(1)}, u32[]{:S(2)}, u32[]{:S(2)}) collective-permute-start(f32[92160]{0:T(1024)S(1)} %pad_maximum_fusion.4), channel_id=1, source_target_pairs={{0,32},{32,0},{1,33},{33,1},{2,34},{34,2},{3,35},{35,3},{4,36},{36... | collective-permute-start | bytes 1105928 | tf_op jit(solution)/shard_map/ppermute | solution.py:106
  93.1 0.0 collective-permute-done
  93.1 0.0 collective-permute-done.1
  93.1 1.0 subtract_multiply_fusion.2
  94.1 0.0 copy-start.6
  94.2 0.0 copy-start.15
  94.4 18.6 %collective-permute-done.2 = f32[92160]{0:T(1024)S(1)} collective-permute-done((f32[92160]{0:T(1024)S(1)}, f32[92160]{0:T(1024)S(1)}, u32[]{:S(2)}, u32[]{:S(2)}) %collective-permute-start.2) | collective-permute-done | bytes 368672 | tf_op jit(solution)/shard_map/ppermute | solution.py:106
  113.0 0.0 copy-done.1
  113.0 0.0 copy-done.2
  113.0 0.2 subtract_multiply_fusion.1
  113.4 2.1 %multiply_subtract_fusion = f32[1,5,8,32,128]{4,3,2,1,0:T(8,128)S(1)} fusion(f32[1,5,8,32,128]{4,3,2,1,0:T(8,128)S(1)} %copy-done, f32[1,5,8,32,127]{4,3,2,1,0:T(8,128)S(1)} %copy-done.6, f32[1,5,8,32,127]{4,3,2,1,0:T(8,128)S(1)} %copy-done.4, f32[1,5,8,31,128]{4,3,2,1,0:T(8,128)S(1)} %copy-done.2, f32[1,5,8,1,128]{4,3,2,1,0:T(1,128)S(1)} %bitcast.74, ...), kind=kLoop, calls=%fused_computation.13 | loop fusion | flops 6881280 | bytes 6183212 | tf_op jit(solution)/shard_map/sub | solution.py:67
  115.6 0.0 copy-start.8
  115.7 0.0 reduce-scatter.2.cloned.1.call-done
  115.7 0.0 copy-done.13
  115.7 0.9 copy-done.8
  116.7 2.0 %fusion.3 = f32[1,5,8,32,128]{4,3,2,1,0:T(8,128)} fusion(f32[1,5,8,32,128]{4,3,2,1,0:T(8,128)S(1)} %copy-done.8, f32[1,5,8,32,128]{4,3,2,1,0:T(8,128)S(1)} %multiply_subtract_fusion, f32[1,5,8,8,128]{4,3,2,1,0:T(8,128)S(1)} %get-tuple-element.50, f32[1,5,8,16,128]{4,3,2,1,0:T(8,128)} %reduce-scatter.2.cloned.1.call-done, ...), kind=kLoop, calls=%fused_computation.12 | loop fusion | flops 819200 | bytes 2752512 | tf_op jit(solution)/shard_map/sub | solution.py:121
  (67 shorter events, 0.4 us)
Async XLA Ops:
  9.4 10.2 %copy-start = (f32[1,5,8,32,128]{4,3,2,1,0:T(8,128)S(1)}, f32[1,5,8,32,128]{4,3,2,1,0:T(8,128)}, u32[]{:S(2)}) copy-start(f32[1,5,8,32,128]{4,3,2,1,0:T(8,128)} %param.7) | copy-start | bytes 1966084
  9.4 75.4 %all-to-all-start = ((f32[8,1,5,8,16,128]{5,4,3,2,1,0:T(8,128)}), f32[8,1,5,8,16,128]{5,4,3,2,1,0:T(8,128)S(1)}, u32[]{:S(2)}, u32[]{:S(2)}) async-start(f32[8,1,5,8,16,128]{5,4,3,2,1,0:T(8,128)} %stack.38), calls=%async_computation | async-start | bytes 5242880 | tf_op jit(solution)/shard_map/all_to_all | solution.py:90
  19.6 96.1 %reduce-scatter.2.cloned.1.call-start = ((), (), s32[]{:S(2)}) async-start(), calls=%async_computation.2 | async-start | bytes 2949120 | tf_op jit(solution)/shard_map/reduce_scatter | solution.py:87
  20.3 72.7 %collective-permute-start = (f32[1,5,1,32,128]{4,3,2,1,0:T(8,128)}, f32[1,5,1,32,128]{4,3,2,1,0:T(8,128)}, u32[]{:S(2)}, u32[]{:S(2)}) collective-permute-start(f32[1,5,1,32,128]{4,3,2,1,0:T(8,128)} %get-tuple-element.42), channel_id=1, source_target_pairs={{1,0},{2,1},{3,2},{4,3},{5,4},{6,5},{7,6},{8,7},{9,8},{10,9},{11,1... | collective-permute-start | bytes 245768 | tf_op jit(solution)/shard_map/ppermute | solution.py:22
  23.8 9.4 %copy-start.17 = (s32[1,2,8,128]{3,2,1,0:T(8,128)S(1)}, s32[1,2,8,128]{3,2,1,0:T(8,128)}, u32[]{:S(2)}) copy-start(s32[1,2,8,128]{3,2,1,0:T(8,128)} %param.13) | copy-start | bytes 24580
  23.8 69.2 %collective-permute-start.1 = (f32[1,5,1,32,128]{4,3,2,1,0:T(8,128)}, f32[1,5,1,32,128]{4,3,2,1,0:T(8,128)}, u32[]{:S(2)}, u32[]{:S(2)}) collective-permute-start(f32[1,5,1,32,128]{4,3,2,1,0:T(8,128)} %get-tuple-element.41), channel_id=1, source_target_pairs={{0,1},{1,2},{2,3},{3,4},{4,5},{5,6},{6,7},{7,8},{8,9},{9,10},{10,1... | collective-permute-start | bytes 245768 | tf_op jit(solution)/shard_map/ppermute | solution.py:19
  26.1 7.9 %copy-start.16 = (f32[8,32,128]{2,1,0:T(8,128)S(1)}, f32[8,32,128]{2,1,0:T(8,128)}, u32[]{:S(2)}) copy-start(f32[8,32,128]{2,1,0:T(8,128)} %param.9) | copy-start | bytes 393220
  26.1 17.4 %collective-permute-start.3 = (f32[1,5,8,16,128]{4,3,2,1,0:T(8,128)}, f32[1,5,8,16,128]{4,3,2,1,0:T(8,128)}, u32[]{:S(2)}, u32[]{:S(2)}) collective-permute-start(f32[1,5,8,16,128]{4,3,2,1,0:T(8,128)} %get-tuple-element.25), channel_id=1, source_target_pairs={{0,32},{32,0},{1,33},{33,1},{2,34},{34,2},{3,35},{35,3},{4,36},{36... | collective-permute-start | bytes 983048 | tf_op jit(solution)/shard_map/ppermute | solution.py:82
  30.7 12.9 %copy-start.7 = (f32[5,8,16,128]{3,2,1,0:T(8,128)S(1)}, f32[5,8,16,128]{3,2,1,0:T(8,128)}, u32[]{:S(2)}) copy-start(f32[5,8,16,128]{3,2,1,0:T(8,128)} %get-tuple-element.24) | copy-start | bytes 983044
  31.1 0.9 copy-start.3
  31.1 2.0 %copy-start.5 = (f32[1,5,8,32,127]{4,3,2,1,0:T(8,128)}, f32[1,5,8,32,127]{4,3,2,1,0:T(8,128)S(1)}, u32[]{:S(2)}) copy-start(f32[1,5,8,32,127]{4,3,2,1,0:T(8,128)S(1)} %get-tuple-element.48) | copy-start | bytes 1950724
  43.6 3.0 %copy-start.14 = (f32[3,5,5]{2,0,1:T(4,128)S(1)}, f32[3,5,5]{2,0,1:T(4,128)}, u32[]{:S(2)}) copy-start(f32[3,5,5]{2,0,1:T(4,128)} %param.11) | copy-start | bytes 904
  84.9 1.6 %copy-start.30 = (s32[2,8,128]{2,1,0:T(8,128)S(1)}, s32[2,8,128]{2,1,0:T(8,128)}, u32[]{:S(2)}) copy-start(s32[2,8,128]{2,1,0:T(8,128)} %param.12) | copy-start | bytes 24580
  84.9 3.0 %copy-start.12 = (f32[2,2,8,128,8]{3,4,2,1,0:T(8,128)S(1)}, f32[2,2,8,128,8]{3,4,2,1,0:T(8,128)}, u32[]{:S(2)}) copy-start(f32[2,2,8,128,8]{3,4,2,1,0:T(8,128)} %compare_convert_fusion) | copy-start | bytes 393220
  88.5 24.5 %copy-start.1 = (f32[1,5,8,31,128]{4,3,2,1,0:T(8,128)S(1)}, f32[1,5,8,31,128]{4,3,2,1,0:T(8,128)}, u32[]{:S(2)}) copy-start(f32[1,5,8,31,128]{4,3,2,1,0:T(8,128)} %get-tuple-element.43) | copy-start | bytes 1904644
  88.5 24.5 %copy-start.2 = (f32[1,5,8,31,128]{4,3,2,1,0:T(8,128)S(1)}, f32[1,5,8,31,128]{4,3,2,1,0:T(8,128)}, u32[]{:S(2)}) copy-start(f32[1,5,8,31,128]{4,3,2,1,0:T(8,128)} %get-tuple-element.44) | copy-start | bytes 1904644
  88.6 24.3 %collective-permute-start.2 = (f32[92160]{0:T(1024)S(1)}, f32[92160]{0:T(1024)S(1)}, u32[]{:S(2)}, u32[]{:S(2)}) collective-permute-start(f32[92160]{0:T(1024)S(1)} %pad_maximum_fusion.4), channel_id=1, source_target_pairs={{0,32},{32,0},{1,33},{33,1},{2,34},{34,2},{3,35},{35,3},{4,36},{36... | collective-permute-start | bytes 1105928 | tf_op jit(solution)/shard_map/ppermute | solution.py:106
  94.1 19.1 %copy-start.4 = (f32[1,5,8,32,127]{4,3,2,1,0:T(8,128)S(1)}, f32[1,5,8,32,127]{4,3,2,1,0:T(8,128)}, u32[]{:S(2)}) copy-start(f32[1,5,8,32,127]{4,3,2,1,0:T(8,128)} %copy-done.3) | copy-start | bytes 1950724
  94.1 19.1 %copy-start.6 = (f32[1,5,8,32,127]{4,3,2,1,0:T(8,128)S(1)}, f32[1,5,8,32,127]{4,3,2,1,0:T(8,128)}, u32[]{:S(2)}) copy-start(f32[1,5,8,32,127]{4,3,2,1,0:T(8,128)} %copy-done.5) | copy-start | bytes 1950724
  94.1 19.1 %copy-start.9 = (f32[8,32,128]{2,1,0:T(8,128)S(1)}, f32[8,32,128]{2,1,0:T(8,128)}, u32[]{:S(2)}) copy-start(f32[8,32,128]{2,1,0:T(8,128)} %get-tuple-element.38) | copy-start | bytes 393220
  94.1 19.1 %copy-start.10 = (f32[8,32,128]{2,1,0:T(8,128)S(1)}, f32[8,32,128]{2,1,0:T(8,128)}, u32[]{:S(2)}) copy-start(f32[8,32,128]{2,1,0:T(8,128)} %get-tuple-element.39) | copy-start | bytes 393220
  94.2 19.1 %copy-start.11 = (f32[8,32,128]{2,1,0:T(8,128)S(1)}, f32[8,32,128]{2,1,0:T(8,128)}, u32[]{:S(2)}) copy-start(f32[8,32,128]{2,1,0:T(8,128)} %get-tuple-element.40) | copy-start | bytes 393220
  94.2 19.1 %copy-start.15 = (f32[8,32,128]{2,1,0:T(8,128)S(1)}, f32[8,32,128]{2,1,0:T(8,128)}, u32[]{:S(2)}) copy-start(f32[8,32,128]{2,1,0:T(8,128)} %param.10) | copy-start | bytes 393220
  94.2 19.1 %copy-start.18 = (f32[5]{0:T(128)S(1)}, f32[5]{0:T(128)}, u32[]{:S(2)}) copy-start(f32[5]{0:T(128)} %get-tuple-element.8) | copy-start | bytes 64
  94.2 19.1 %copy-start.19 = (f32[5]{0:T(128)S(1)}, f32[5]{0:T(128)}, u32[]{:S(2)}) copy-start(f32[5]{0:T(128)} %get-tuple-element.9) | copy-start | bytes 64
  94.2 19.1 %copy-start.20 = (f32[5]{0:T(128)S(1)}, f32[5]{0:T(128)}, u32[]{:S(2)}) copy-start(f32[5]{0:T(128)} %get-tuple-element.10) | copy-start | bytes 64
  94.2 19.1 %copy-start.21 = (f32[5]{0:T(128)S(1)}, f32[5]{0:T(128)}, u32[]{:S(2)}) copy-start(f32[5]{0:T(128)} %get-tuple-element.11) | copy-start | bytes 64
  94.2 19.1 %copy-start.22 = (f32[5]{0:T(128)S(1)}, f32[5]{0:T(128)}, u32[]{:S(2)}) copy-start(f32[5]{0:T(128)} %get-tuple-element.12) | copy-start | bytes 64
  94.2 19.1 %copy-start.23 = (f32[5]{0:T(128)S(1)}, f32[5]{0:T(128)}, u32[]{:S(2)}) copy-start(f32[5]{0:T(128)} %get-tuple-element.13) | copy-start | bytes 64
  94.2 19.1 %copy-start.24 = (f32[5]{0:T(128)S(1)}, f32[5]{0:T(128)}, u32[]{:S(2)}) copy-start(f32[5]{0:T(128)} %get-tuple-element.14) | copy-start | bytes 64
  94.2 19.1 %copy-start.25 = (f32[5]{0:T(128)S(1)}, f32[5]{0:T(128)}, u32[]{:S(2)}) copy-start(f32[5]{0:T(128)} %get-tuple-element.15) | copy-start | bytes 64
  94.3 19.1 %copy-start.26 = (f32[5]{0:T(128)S(1)}, f32[5]{0:T(128)}, u32[]{:S(2)}) copy-start(f32[5]{0:T(128)} %get-tuple-element.16) | copy-start | bytes 64
  94.3 19.1 %copy-start.27 = (f32[5]{0:T(128)S(1)}, f32[5]{0:T(128)}, u32[]{:S(2)}) copy-start(f32[5]{0:T(128)} %get-tuple-element.17) | copy-start | bytes 64
  94.3 19.1 %copy-start.28 = (f32[5]{0:T(128)S(1)}, f32[5]{0:T(128)}, u32[]{:S(2)}) copy-start(f32[5]{0:T(128)} %get-tuple-element.18) | copy-start | bytes 64
  94.3 19.1 %copy-start.29 = (f32[5]{0:T(128)S(1)}, f32[5]{0:T(128)}, u32[]{:S(2)}) copy-start(f32[5]{0:T(128)} %get-tuple-element.19) | copy-start | bytes 64
  113.4 2.3 %copy-start.13 = (f32[8,32,128]{2,1,0:T(8,128)S(1)}, f32[8,32,128]{2,1,0:T(8,128)}, u32[]{:S(2)}) copy-start(f32[8,32,128]{2,1,0:T(8,128)} %broadcast_multiply_fusion) | copy-start | bytes 393220
  115.6 1.1 copy-start.8
Sparse Core Ops, SparseCore 0:
  46.7 59.4 reduce-scatter.1
